TPU v7x, 32 devices: a whole 2x2x4 slice. The times are simulated.
32 devices in a mesh: group: 2 (over y), head: 4 (over x, core), seq: 4 (over z).
Axes of the slice: x: 2, y: 2, z: 4, core: 2. Of those that a mesh axis runs over, the one named last changes fastest.
Arguments:
- new_queries: bfloat16 [512, 4096], P(('group', 'seq'), 'head'), parts along dimension 0, may hold values from -80 to 80
- new_keys: bfloat16 [512, 1024], P(('group', 'seq'), 'head'), parts along dimension 0, may hold values from -6 to 6
- new_values: bfloat16 [512, 1024], P(('group', 'seq'), 'head'), parts along dimension 0, may hold values from -6 to 6
- cache_keys: bfloat16 [8192, 1024], P(('group', 'seq'), 'head'), parts along dimension 0, may hold values from -5 to 5
- cache_values: bfloat16 [8192, 1024], P(('group', 'seq'), 'head'), parts along dimension 0, may hold values from -6 to 6
- segment_ids: int32 [512], P('group'), parts along dimension 0, may hold values from 0 to 7, as said below
- cache_length: int32 [2], P('group'), parts along dimension 0, may hold values from 512 to 4096
Outputs:
- attended: bfloat16 [512, 4096], P(('group', 'seq'), 'head'), parts along dimension 0
There are 2 independent parts, one for each index of `group`. A program takes and returns all parts, laid end to end along the dimension named above; each array names one. Nothing has to cross between parts.
Inputs may be any that keep to these rules, and one draw needn't show every extreme that they name: `segment_ids`: Non-decreasing along the positions; every number of 0 to 7 appears.
All inputs are finite; a program needn't handle non-finite values.
Results may differ from a plain program's by a relative error of at most 0.0024.
Values may be sent and summed in bfloat16 or wider, within the bound.
No kernel may reach another device: no remote copies, remote signals or barrier semaphores. Data moves between devices by JAX's collectives and lax.ppermute only.
A program may use at most 64 MiB of HBM per device.

v0:
```python
import jax
import jax.numpy as jnp
from jax import lax
from jax.sharding import PartitionSpec as P

HEAD_DIM = 128
NEG_FILL = -1e30


def on_device(
    new_queries, new_keys, new_values, cache_keys, cache_values, segment_ids, cache_length
):
    head_size = HEAD_DIM
    own_count = new_queries.shape[0]
    join_rows = segment_ids.shape[0]
    cache_rows = cache_keys.shape[0]
    heads_kv = cache_keys.shape[1] // head_size
    heads_q = new_queries.shape[1] // head_size
    group_size = heads_q // heads_kv
    seq_count = lax.axis_size("seq")
    seq_rank = lax.axis_index("seq")
    score_scale = head_size ** (-0.5)
    cache_limit = cache_length[0]
    all_queries, all_keys, all_values = (
        lax.all_gather(new_queries, "seq", axis=0, tiled=True),
        lax.all_gather(new_keys, "seq", axis=0, tiled=True),
        lax.all_gather(new_values, "seq", axis=0, tiled=True),
    )
    keys_here, values_here = (cache_keys, cache_values)
    live_rows = jnp.clip(cache_limit - seq_rank * cache_rows, 0, cache_rows)
    tile_width = min(cache_rows // seq_count, 256)
    block_rows = min(256, cache_rows)
    tiles_per_block = block_rows // tile_width
    block_total = (live_rows + block_rows - 1) // block_rows
    keys_tiled = keys_here.reshape(cache_rows, heads_kv, head_size)
    values_tiled = values_here.reshape(cache_rows, heads_kv, head_size)
    query_block = min(64, join_rows)
    grouped = all_queries.reshape(
        join_rows // query_block, query_block, heads_kv, group_size, head_size
    )

    def one_block(block_queries):

        def step_pass(block_index, running):
            best, numer_acc, denom_acc = running
            start = block_index * block_rows
            key_tile = lax.dynamic_slice_in_dim(keys_tiled, start, block_rows, 0)
            scores = (
                jnp.einsum(
                    "cgrd,tgd->cgrt", block_queries, key_tile, preferred_element_type=jnp.float32
                )
                * score_scale
            )
            usable = (start + jnp.arange(block_rows, dtype=jnp.int32) < live_rows).reshape(
                tiles_per_block, tile_width
            )
            split = scores.reshape(query_block, heads_kv, group_size, tiles_per_block, tile_width)
            tile_max = jnp.max(jnp.where(usable, split, NEG_FILL), axis=-1)
            weights = jnp.exp(jnp.where(usable, split - tile_max[..., None], NEG_FILL)).astype(
                jnp.bfloat16
            )
            value_tile = lax.dynamic_slice_in_dim(values_tiled, start, block_rows, 0).reshape(
                tiles_per_block, tile_width, heads_kv, head_size
            )
            tile_numer = jnp.einsum(
                "cgrbt,btgd->cgrbd", weights, value_tile, preferred_element_type=jnp.float32
            )
            tile_denom = jnp.sum(weights.astype(jnp.float32), axis=-1)
            new_best = jnp.maximum(best, jnp.max(tile_max, axis=-1))
            keep = jnp.exp(best - new_best)
            factor = jnp.exp(tile_max - new_best[..., None])
            numer_acc = numer_acc * keep[..., None] + jnp.sum(
                tile_numer * factor[..., None], axis=3
            )
            denom_acc = denom_acc * keep + jnp.sum(tile_denom * factor, axis=-1)
            return (new_best, numer_acc, denom_acc)

        start_state = (
            jnp.full((query_block, heads_kv, group_size), NEG_FILL, jnp.float32),
            jnp.zeros((query_block, heads_kv, group_size, head_size), jnp.float32),
            jnp.zeros((query_block, heads_kv, group_size), jnp.float32),
        )
        return lax.fori_loop(0, block_total, step_pass, start_state)

    block_best, block_numer, block_denom = lax.map(one_block, grouped)
    cache_max = block_best.reshape(join_rows, heads_kv, group_size)
    cache_numer = block_numer.reshape(join_rows, heads_kv, group_size, head_size)
    cache_denom = block_denom.reshape(join_rows, heads_kv, group_size)
    own_queries = new_queries.reshape(own_count, heads_kv, group_size, head_size)
    fresh_scores = (
        jnp.einsum(
            "cgrd,tgd->cgrt",
            own_queries,
            all_keys.reshape(join_rows, heads_kv, head_size),
            preferred_element_type=jnp.float32,
        )
        * score_scale
    )
    start_row = seq_rank * own_count
    own_positions = start_row + jnp.arange(own_count, dtype=jnp.int32)
    own_segments = lax.dynamic_slice_in_dim(segment_ids, start_row, own_count, 0)
    key_positions = jnp.arange(join_rows, dtype=jnp.int32)
    allowed = (key_positions[None, :] <= own_positions[:, None]) & (
        segment_ids[None, :] == own_segments[:, None]
    )
    allowed = allowed[:, None, None, :]
    fresh_max = jnp.max(jnp.where(allowed, fresh_scores, NEG_FILL), axis=-1)
    zero_index = jnp.zeros((), jnp.int32)
    merged = lax.dynamic_update_slice(
        cache_max,
        jnp.maximum(lax.dynamic_slice_in_dim(cache_max, start_row, own_count, 0), fresh_max),
        (start_row, zero_index, zero_index),
    )
    row_max = (
        lax.pmax(merged.reshape(join_rows, heads_q).astype(jnp.bfloat16), "seq")
        .astype(jnp.float32)
        .reshape(join_rows, heads_kv, group_size)
    )
    rescale = jnp.exp(cache_max - row_max)
    scaled_numer = (cache_numer * rescale[..., None]).reshape(join_rows, heads_q * head_size)
    scaled_denom = (cache_denom * rescale).reshape(join_rows, heads_q)
    own_numer, own_denom = (
        lax.psum_scatter(scaled_numer, "seq", scatter_dimension=0, tiled=True),
        lax.psum_scatter(scaled_denom, "seq", scatter_dimension=0, tiled=True),
    )
    own_max = lax.dynamic_slice_in_dim(row_max, start_row, own_count, 0)
    fresh_weights = jnp.exp(
        jnp.where(allowed, fresh_scores - fresh_max[..., None], NEG_FILL)
    ).astype(jnp.bfloat16)
    fresh_factor = jnp.exp(fresh_max - own_max)
    fresh_numer = (
        jnp.einsum(
            "cgrt,tgd->cgrd",
            fresh_weights,
            all_values.reshape(join_rows, heads_kv, head_size),
            preferred_element_type=jnp.float32,
        )
        * fresh_factor[..., None]
    )
    fresh_denom = jnp.sum(fresh_weights.astype(jnp.float32), axis=-1) * fresh_factor
    total_numer = own_numer + fresh_numer.reshape(own_count, heads_q * head_size)
    total_denom = own_denom + fresh_denom.reshape(own_count, heads_q)
    attended = total_numer.reshape(own_count, heads_q, head_size) / total_denom[..., None]
    return attended.reshape(own_count, heads_q * head_size).astype(jnp.bfloat16)


def solution(mesh):
    placed = (
        P(("group", "seq"), "head"),
        P(("group", "seq"), "head"),
        P(("group", "seq"), "head"),
        P(("group", "seq"), "head"),
        P(("group", "seq"), "head"),
        P("group"),
        P("group"),
    )
    return jax.shard_map(
        on_device,
        mesh=mesh,
        in_specs=placed,
        out_specs=P(("group", "seq"), "head"),
        check_vma=False,
    )
```

profile of v0, /device:TPU:0, one launch (start us, length us, event | category | flops | bytes accessed | tf_op | source)
XLA Modules:
  0.0 127.6 jit_solution(12809682222911493052)
XLA Ops:
  7.2 17.6 %all_gather.9 = bf16[256,1024]{1,0:T(8,128)(2,1)S(1)} all-gather(bf16[64,1024]{1,0:T(8,128)(2,1)} %param.11), channel_id=1, replica_groups=mesh['group'=2,'head'=4,'seq'=4] {'seq'}, dimensions={0}, use_global_device_ids=true | all-gather | bytes 655360 | tf_op jit(solution)/shard_map/all_gather | solution.py:25
  24.8 0.4 reshape.144
  25.2 0.7 copy-done.1
  26.3 1.3 copy.30
  27.9 18.3 %while.29 = (s32[]{:T(128)}, f32[4,64,2,4]{1,0,3,2:T(4,128)S(1)}, f32[4,64,2,4,128]{4,3,2,1,0:T(4,128)S(1)}, f32[4,64,2,4]{1,0,3,2:T(4,128)S(1)}, bf16[4,64,2,4,...) while((s32[]{:T(128)}, f32[4,64,2,4]{1,0,3,2:T(4,128)S(1)}, ...), condition=%wide.region_5.6_spmd, body=%wide.region_0.5_spmd.sunk | while | flops 68749824 | bytes 3850228 | solution.py:85
  28.0 4.1 %while.30 = (s32[]{:T(128)}, f32[64,2,4]{0,2,1:T(4,128)S(1)}, f32[64,2,4,128]{3,0,2,1:T(8,128)S(1)}, f32[64,2,4]{0,2,1:T(4,128)S(1)}, s32[]{:T(128)}, /*index=5*...) while((s32[]{:T(128)}, f32[64,2,4]{0,2,1:T(4,128)S(1)}, ...), condition=%wide.region_4.4_spmd, body=%wide.region_1.3_spmd.sunk | while | flops 68749824 | bytes 2526915 | solution.py:83
  28.1 0.3 select_reduce_fusion.3
  28.4 0.3 convert_reduce_fusion.3
  28.7 0.3 fusion.26
  29.1 0.3 select_reduce_fusion.3
  29.4 0.3 convert_reduce_fusion.3
  29.7 0.4 fusion.26
  30.1 0.3 select_reduce_fusion.3
  30.4 0.3 convert_reduce_fusion.3
  30.7 0.3 fusion.26
  31.1 0.3 select_reduce_fusion.3
  31.5 0.3 convert_reduce_fusion.3
  31.8 0.4 fusion.26
  32.6 4.1 %while.30 = (s32[]{:T(128)}, f32[64,2,4]{0,2,1:T(4,128)S(1)}, f32[64,2,4,128]{3,0,2,1:T(8,128)S(1)}, f32[64,2,4]{0,2,1:T(4,128)S(1)}, s32[]{:T(128)}, /*index=5*...) while((s32[]{:T(128)}, f32[64,2,4]{0,2,1:T(4,128)S(1)}, ...), condition=%wide.region_4.4_spmd, body=%wide.region_1.3_spmd.sunk | while | flops 68749824 | bytes 2526915 | solution.py:83
  32.6 0.3 select_reduce_fusion.3
  33.3 0.4 fusion.26
  33.6 0.3 select_reduce_fusion.3
  34.3 0.3 fusion.26
  34.7 0.3 select_reduce_fusion.3
  35.3 0.4 fusion.26
  35.7 0.3 select_reduce_fusion.3
  36.3 0.3 fusion.26
  37.1 4.1 %while.30 = (s32[]{:T(128)}, f32[64,2,4]{0,2,1:T(4,128)S(1)}, f32[64,2,4,128]{3,0,2,1:T(8,128)S(1)}, f32[64,2,4]{0,2,1:T(4,128)S(1)}, s32[]{:T(128)}, /*index=5*...) while((s32[]{:T(128)}, f32[64,2,4]{0,2,1:T(4,128)S(1)}, ...), condition=%wide.region_4.4_spmd, body=%wide.region_1.3_spmd.sunk | while | flops 68749824 | bytes 2526915 | solution.py:83
  37.2 0.3 select_reduce_fusion.3
  37.5 0.3 convert_reduce_fusion.3
  37.8 0.4 fusion.26
  38.2 0.3 select_reduce_fusion.3
  38.5 0.3 convert_reduce_fusion.3
  38.8 0.3 fusion.26
  39.2 0.3 select_reduce_fusion.3
  39.9 0.4 fusion.26
  40.3 0.3 select_reduce_fusion.3
  40.9 0.3 fusion.26
  41.7 4.1 %while.30 = (s32[]{:T(128)}, f32[64,2,4]{0,2,1:T(4,128)S(1)}, f32[64,2,4,128]{3,0,2,1:T(8,128)S(1)}, f32[64,2,4]{0,2,1:T(4,128)S(1)}, s32[]{:T(128)}, /*index=5*...) while((s32[]{:T(128)}, f32[64,2,4]{0,2,1:T(4,128)S(1)}, ...), condition=%wide.region_4.4_spmd, body=%wide.region_1.3_spmd.sunk | while | flops 68749824 | bytes 2526915 | solution.py:83
  41.7 0.3 select_reduce_fusion.3
  42.4 0.4 fusion.26
  42.8 0.3 select_reduce_fusion.3
  43.4 0.3 fusion.26
  43.8 0.3 select_reduce_fusion.3
  44.4 0.4 fusion.26
  44.8 0.3 select_reduce_fusion.3
  45.5 0.3 fusion.26
  46.5 0.7 copy-done.3
  47.1 13.3 %all_gather.10 = bf16[256,256]{1,0:T(8,128)(2,1)S(1)} all-gather(bf16[64,256]{1,0:T(8,128)(2,1)S(1)} %copy-done.3), channel_id=1, replica_groups=mesh['group'=2,'head'=4,'seq'=4] {'seq'}, dimensions={0}, use_global_device_ids=true | all-gather | bytes 163840 | tf_op jit(solution)/shard_map/all_gather | solution.py:26
  60.6 0.7 copy-done.5
  61.4 0.3 select_reduce_fusion.1
  62.0 8.7 %pmax.7 = bf16[256,8]{0,1:T(8,128)(2,1)S(1)} all-reduce(bf16[256,8]{0,1:T(8,128)(2,1)S(1)} %convert_element_type.27), channel_id=1, replica_groups=mesh['group'=2,'head'=4,'seq'=4] {'seq'}, use_global_device_ids=true, to_apply=%region_7.8 | all-reduce | flops 2048 | bytes 8192 | tf_op jit(solution)/shard_map/pmax | solution.py:115
  70.7 0.8 copy.54
  71.6 0.4 reshape.147
  72.2 1.6 %mul.74 = f32[256,2,4,128]{3,2,1,0:T(4,128)} broadcast(f32[256,2,4]{2,1,0:T(2,128)S(1)} %copy.39), dimensions={0,1,2} | broadcast | bytes 1056768 | tf_op jit(solution)/shard_map/mul | solution.py:120
  73.8 1.6 %mul.75 = f32[256,1024]{1,0:T(8,128)S(1)} reshape(f32[256,2,4,128]{3,2,1,0:T(4,128)} %mul.74) | data formatting | bytes 2097152 | tf_op jit(solution)/shard_map/mul | solution.py:120
  75.4 1.2 mul.76
  76.6 0.7 copy-done.4
  77.3 13.5 %all_gather.11 = bf16[256,256]{1,0:T(8,128)(2,1)S(1)} all-gather(bf16[64,256]{1,0:T(8,128)(2,1)S(1)} %copy-done.4), channel_id=1, replica_groups=mesh['group'=2,'head'=4,'seq'=4] {'seq'}, dimensions={0}, use_global_device_ids=true | all-gather | bytes 163840 | tf_op jit(solution)/shard_map/all_gather | solution.py:27
  91.3 0.3 fusion.12
  92.0 0.8 copy.55
  92.9 26.2 %reduce-scatter.5.cloned.1.call-done = f32[64,1024]{1,0:T(8,128)} async-done(((f32[256,1024]{1,0:T(8,128)}), f32[64,1024]{1,0:T(8,128)}) %reduce-scatter.5.cloned.1.call-update) | async-done | bytes 262160 | tf_op jit(solution)/shard_map/reduce_scatter | solution.py:123
  119.2 0.8 copy-done.2
  120.0 0.7 fusion.13
  (117 shorter events, 7.5 us)
Async XLA Ops:
  6.5 85.4 %reduce-scatter.7.cloned.1.call-start = ((), (), s32[]{:S(2)}) async-start(), calls=%async_computation.3 | async-start | bytes 163840
  24.8 1.0 copy-start.1
  27.9 18.4 %copy-start = (bf16[64,1024]{1,0:T(8,128)(2,1)S(1)}, bf16[64,1024]{1,0:T(8,128)(2,1)}, u32[]{:S(2)}) copy-start(bf16[64,1024]{1,0:T(8,128)(2,1)} %param.11) | copy-start | bytes 393220
  46.4 0.8 copy-start.3
  60.6 0.7 copy-start.5
  71.5 47.6 %reduce-scatter.5.cloned.1.call-start = ((), (), s32[]{:S(2)}) async-start(), calls=%async_computation.2 | async-start | bytes 1310720 | tf_op jit(solution)/shard_map/reduce_scatter | solution.py:123
  76.6 0.8 copy-start.4
  119.1 0.9 copy-start.2
Sparse Core Ops, SparseCore 0:
  71.6 19.7 reduce-scatter.6
  93.8 25.1 reduce-scatter.4
where the time goes:
time: 128 us
  blocking collectives  53.1 us (41%)
  waiting for transfers between devices  26.3 us (21%)
  between operations  14.3 us (11%)
  local copies, waits for them, and re-layouts  14.1 us (11%)
  matrix products  11.4 us (9%)
  other arithmetic  7.33 us (6%)
    reduce_scatter x1, waiting for transfers between devices, on_device(): lax.psum_scatter(scaled_numer, 'seq', scatter_dimension=0, tiled=True)  26.2 us
    all_gather x1, blocking collectives, on_device(): lax.all_gather(new_queries, 'seq', axis=0, tiled=True)  17.6 us
    all_gather x1, blocking collectives, on_device(): lax.all_gather(new_values, 'seq', axis=0, tiled=True)  13.5 us
    all_gather x1, blocking collectives, on_device(): lax.all_gather(new_keys, 'seq', axis=0, tiled=True)  13.3 us
    pmax x1, blocking collectives, on_device(): lax.pmax(merged.reshape(join_rows, heads_q).astype(jnp.bfloat16), 'seq')  8.67 us
    unnamed x17, local copies, waits for them, and re-layouts  6.63 us
    dot_general x16, matrix products, step_pass(): jnp.einsum('cgrbt,btgd->cgrbd', weights, value_tile, preferred_element_ty...  5.59 us
    dot_general x16, matrix products, step_pass(): jnp.einsum('cgrd,tgd->cgrt', block_queries, key_tile, preferred_element_t...  5.24 us
  transfers between devices with their start and end apart: 2, of which 1 were waited for; matrix products, arithmetic and copies ran while one was open for 5% of the time, Pallas kernels for 0%

commit v1 on v0

--- a/solution.py
+++ b/solution.py
@@ -5,6 +5,18 @@
 
 HEAD_DIM = 128
 NEG_FILL = -1e30
+
+
+def collect(value, axis, dim):
+    ways, here, turn = (lax.axis_size(axis), lax.axis_index(axis), value.shape[dim])
+    line, have = (value, 1)
+    while have < ways:
+        line = jnp.concatenate(
+            [line, lax.ppermute(line, axis, [(d, (d - have) % ways) for d in range(ways)])],
+            axis=dim,
+        )
+        have = 2 * have
+    return jnp.roll(line, here * turn, axis=dim)
 
 
 def on_device(
@@ -22,7 +34,7 @@
     score_scale = head_size ** (-0.5)
     cache_limit = cache_length[0]
     all_queries, all_keys, all_values = (
-        lax.all_gather(new_queries, "seq", axis=0, tiled=True),
+        collect(new_queries, "seq", 0),
         lax.all_gather(new_keys, "seq", axis=0, tiled=True),
         lax.all_gather(new_values, "seq", axis=0, tiled=True),
     )

time: 128 us -> 124 us (0.969)
  blocking collectives: 53.1 us -> 35.4 us
  starting transfers between devices: 0.04 us -> 5.81 us
  waiting for transfers between devices: 26.3 us -> 31 us
  local copies, waits for them, and re-layouts: 14.1 us -> 17.5 us
    all_gather x1 -> x0, blocking collectives: 17.6 us -> none  [on_device(): lax.all_gather(new_queries, 'seq', axis=0, tiled=True)]
    ppermute x0 -> x2, waiting for transfers between devices: none -> 6.66 us  [collect(): lax.ppermute(line, axis, [(d, (d - have) % ways) for d in range(ways)])]
    ppermute x0 -> x2, starting transfers between devices: none -> 5.76 us  [collect(): lax.ppermute(line, axis, [(d, (d - have) % ways) for d in range(ways)])]
    dynamic_update_slice x12, local copies, waits for them, and re-layouts: 1.12 us -> 3.81 us  [on_device(): block_best, block_numer, block_denom = lax.map(one_block, grouped)]
    reduce_scatter x1, waiting for transfers between devices: 26.2 us -> 24.3 us  [on_device(): lax.psum_scatter(scaled_numer, 'seq', scatter_dimension=0, tiled=True)]
    unnamed x17 -> x24, local copies, waits for them, and re-layouts: 6.63 us -> 5.08 us
  transfers between devices with their start and end apart: 2 -> 4, of which waited for: 1 -> 2; matrix products, arithmetic and copies ran while one was open for 5% -> 9% of each run, Pallas kernels for 0% -> 0%
where the time goes in v1:
time: 124 us
  blocking collectives  35.4 us (29%)
  waiting for transfers between devices  31 us (25%)
  local copies, waits for them, and re-layouts  17.5 us (14%)
  between operations  14.4 us (12%)
  matrix products  11.4 us (9%)
  other arithmetic  7.33 us (6%)
  starting transfers between devices  5.81 us (5%)
    reduce_scatter x1, waiting for transfers between devices, on_device(): lax.psum_scatter(scaled_numer, 'seq', scatter_dimension=0, tiled=True)  24.3 us
    all_gather x1, blocking collectives, on_device(): lax.all_gather(new_keys, 'seq', axis=0, tiled=True)  13.6 us
    all_gather x1, blocking collectives, on_device(): lax.all_gather(new_values, 'seq', axis=0, tiled=True)  13.5 us
    pmax x1, blocking collectives, on_device(): lax.pmax(merged.reshape(join_rows, heads_q).astype(jnp.bfloat16), 'seq')  8.38 us
    ppermute x2, waiting for transfers between devices, collect(): lax.ppermute(line, axis, [(d, (d - have) % ways) for d in range(ways)])  6.66 us
    ppermute x2, starting transfers between devices, collect(): lax.ppermute(line, axis, [(d, (d - have) % ways) for d in range(ways)])  5.76 us
    dot_general x16, matrix products, step_pass(): jnp.einsum('cgrbt,btgd->cgrbd', weights, value_tile, preferred_element_ty...  5.59 us
    dot_general x16, matrix products, step_pass(): jnp.einsum('cgrd,tgd->cgrt', block_queries, key_tile, preferred_element_t...  5.24 us
  transfers between devices with their start and end apart: 4, of which 2 were waited for; matrix products, arithmetic and copies ran while one was open for 9% of the time, Pallas kernels for 0%

profile of v1, /device:TPU:0, one launch (start us, length us, event | category | flops | bytes accessed | tf_op | source)
XLA Modules:
  0.0 123.9 jit_solution(9972568941000846922)
XLA Ops:
  6.5 5.0 %collective-permute-start = (bf16[64,1024]{1,0:T(8,128)(2,1)}, bf16[64,1024]{1,0:T(8,128)(2,1)S(1)}, u32[]{:S(2)}, u32[]{:S(2)}) collective-permute-start(bf16[64,1024]{1,0:T(8,128)(2,1)} %param.11), channel_id=1, source_target_pairs={{0,3},{1,0},{2,1},{3,2},{4,7},{5,4},{6,5},{7,6},{8,11},{9,8},{10,9... | collective-permute-start | bytes 393224 | tf_op jit(solution)/shard_map/ppermute | solution.py:15
  11.6 1.0 reshape.150
  12.6 13.6 %all_gather.6 = bf16[256,256]{1,0:T(8,128)(2,1)S(1)} all-gather(bf16[64,256]{1,0:T(8,128)(2,1)S(1)} %copy-done.4), channel_id=1, replica_groups=mesh['group'=2,'head'=4,'seq'=4] {'seq'}, dimensions={0}, use_global_device_ids=true | all-gather | bytes 163840 | tf_op jit(solution)/shard_map/all_gather | solution.py:38
  26.3 0.7 copy-done.6
  27.2 0.7 collective-permute-start.1
  27.9 0.3 select_reduce_fusion.1
  29.5 0.8 copy-done.2
  30.8 6.7 %collective-permute-done.1 = bf16[128,1024]{1,0:T(8,128)(2,1)S(1)} collective-permute-done((bf16[128,1024]{1,0:T(8,128)(2,1)S(1)}, bf16[128,1024]{1,0:T(8,128)(2,1)S(1)}, u32[]{:S(2)}, u32[]{:S(2)}) %collective-permute-start.1) | collective-permute-done | bytes 262176 | tf_op jit(solution)/shard_map/ppermute | solution.py:15
  37.6 0.4 reshape.144
  37.9 20.9 %while.29 = (s32[]{:T(128)}, f32[4,64,2,4]{1,0,3,2:T(4,128)S(1)}, f32[4,64,2,4,128]{4,3,2,1,0:T(4,128)}, f32[4,64,2,4]{1,0,3,2:T(4,128)S(1)}, bf16[4,64,2,4,128]...) while((s32[]{:T(128)}, f32[4,64,2,4]{1,0,3,2:T(4,128)S(1)}, ...), condition=%wide.region_5.6_spmd, body=%wide.region_0.5_spmd.sunk | while | flops 68749824 | bytes 3850228 | solution.py:97
  38.1 4.1 %while.30 = (s32[]{:T(128)}, f32[64,2,4]{0,2,1:T(4,128)S(1)}, f32[64,2,4,128]{3,0,2,1:T(8,128)S(1)}, f32[64,2,4]{0,2,1:T(4,128)S(1)}, s32[]{:T(128)}, /*index=5*...) while((s32[]{:T(128)}, f32[64,2,4]{0,2,1:T(4,128)S(1)}, ...), condition=%wide.region_4.4_spmd, body=%wide.region_1.3_spmd.sunk | while | flops 68749824 | bytes 2526915 | solution.py:95
  38.1 0.3 select_reduce_fusion.3
  38.8 0.4 fusion.26
  39.2 0.3 select_reduce_fusion.3
  39.8 0.3 fusion.26
  40.2 0.3 select_reduce_fusion.3
  40.5 0.3 convert_reduce_fusion.3
  40.8 0.4 fusion.26
  41.2 0.3 select_reduce_fusion.3
  41.8 0.3 fusion.26
  42.2 0.9 copy_dynamic-update-slice_fusion.2
  43.3 4.1 %while.30 = (s32[]{:T(128)}, f32[64,2,4]{0,2,1:T(4,128)S(1)}, f32[64,2,4,128]{3,0,2,1:T(8,128)S(1)}, f32[64,2,4]{0,2,1:T(4,128)S(1)}, s32[]{:T(128)}, /*index=5*...) while((s32[]{:T(128)}, f32[64,2,4]{0,2,1:T(4,128)S(1)}, ...), condition=%wide.region_4.4_spmd, body=%wide.region_1.3_spmd.sunk | while | flops 68749824 | bytes 2526915 | solution.py:95
  43.3 0.3 select_reduce_fusion.3
  44.0 0.3 fusion.26
  44.4 0.3 select_reduce_fusion.3
  45.0 0.4 fusion.26
  45.4 0.3 select_reduce_fusion.3
  46.0 0.3 fusion.26
  46.4 0.3 select_reduce_fusion.3
  47.1 0.4 fusion.26
  47.5 0.9 copy_dynamic-update-slice_fusion.2
  48.5 4.1 %while.30 = (s32[]{:T(128)}, f32[64,2,4]{0,2,1:T(4,128)S(1)}, f32[64,2,4,128]{3,0,2,1:T(8,128)S(1)}, f32[64,2,4]{0,2,1:T(4,128)S(1)}, s32[]{:T(128)}, /*index=5*...) while((s32[]{:T(128)}, f32[64,2,4]{0,2,1:T(4,128)S(1)}, ...), condition=%wide.region_4.4_spmd, body=%wide.region_1.3_spmd.sunk | while | flops 68749824 | bytes 2526915 | solution.py:95
  48.6 0.3 select_reduce_fusion.3
  49.2 0.4 fusion.26
  49.6 0.3 select_reduce_fusion.3
  50.2 0.3 fusion.26
  50.6 0.3 select_reduce_fusion.3
  51.3 0.4 fusion.26
  51.7 0.3 select_reduce_fusion.3
  52.3 0.3 fusion.26
  52.7 0.9 copy_dynamic-update-slice_fusion.2
  53.8 4.1 %while.30 = (s32[]{:T(128)}, f32[64,2,4]{0,2,1:T(4,128)S(1)}, f32[64,2,4,128]{3,0,2,1:T(8,128)S(1)}, f32[64,2,4]{0,2,1:T(4,128)S(1)}, s32[]{:T(128)}, /*index=5*...) while((s32[]{:T(128)}, f32[64,2,4]{0,2,1:T(4,128)S(1)}, ...), condition=%wide.region_4.4_spmd, body=%wide.region_1.3_spmd.sunk | while | flops 68749824 | bytes 2526915 | solution.py:95
  53.8 0.3 select_reduce_fusion.3
  54.4 0.3 fusion.26
  54.8 0.3 select_reduce_fusion.3
  55.5 0.4 fusion.26
  55.9 0.3 select_reduce_fusion.3
  56.5 0.3 fusion.26
  56.9 0.3 select_reduce_fusion.3
  57.5 0.4 fusion.26
  57.9 0.9 copy_dynamic-update-slice_fusion.2
  59.3 8.4 %pmax.7 = bf16[256,8]{0,1:T(8,128)(2,1)S(1)} all-reduce(bf16[256,8]{0,1:T(8,128)(2,1)S(1)} %convert_element_type.27), channel_id=1, replica_groups=mesh['group'=2,'head'=4,'seq'=4] {'seq'}, use_global_device_ids=true, to_apply=%region_7.8 | all-reduce | flops 2048 | bytes 8192 | tf_op jit(solution)/shard_map/pmax | solution.py:127
  67.7 0.8 copy.54
  68.6 1.6 %reshape.147 = f32[256,1024]{1,0:T(8,128)S(1)} reshape(f32[4,64,2,4,128]{4,3,2,1,0:T(4,128)} %get-tuple-element.104) | data formatting | bytes 2097152 | tf_op jit(solution)/shard_map/reshape | solution.py:99
  70.4 1.6 %mul.75 = f32[256,2,4,128]{3,2,1,0:T(4,128)} broadcast(f32[256,2,4]{2,1,0:T(2,128)S(1)} %copy.39), dimensions={0,1,2} | broadcast | bytes 1056768 | tf_op jit(solution)/shard_map/mul | solution.py:132
  72.0 1.6 %mul.76 = f32[256,1024]{1,0:T(8,128)S(1)} reshape(f32[256,2,4,128]{3,2,1,0:T(4,128)} %mul.75) | data formatting | bytes 2097152 | tf_op jit(solution)/shard_map/mul | solution.py:132
  73.7 1.1 mul.77
  74.8 0.7 copy-done.5
  75.6 13.5 %all_gather.7 = bf16[256,256]{1,0:T(8,128)(2,1)S(1)} all-gather(bf16[64,256]{1,0:T(8,128)(2,1)S(1)} %copy-done.5), channel_id=1, replica_groups=mesh['group'=2,'head'=4,'seq'=4] {'seq'}, dimensions={0}, use_global_device_ids=true | all-gather | bytes 163840 | tf_op jit(solution)/shard_map/all_gather | solution.py:39
  89.5 0.3 fusion.12
  90.2 0.8 copy.55
  91.1 24.3 %reduce-scatter.5.cloned.1.call-done = f32[64,1024]{1,0:T(8,128)} async-done(((f32[256,1024]{1,0:T(8,128)}), f32[64,1024]{1,0:T(8,128)}) %reduce-scatter.5.cloned.1.call-update) | async-done | bytes 262160 | tf_op jit(solution)/shard_map/reduce_scatter | solution.py:135
  115.5 0.8 copy-done.3
  116.3 0.7 fusion.13
  (130 shorter events, 8.4 us)
Async XLA Ops:
  6.5 83.6 %reduce-scatter.7.cloned.1.call-start = ((), (), s32[]{:S(2)}) async-start(), calls=%async_computation.3 | async-start | bytes 163840
  6.5 20.6 %collective-permute-start = (bf16[64,1024]{1,0:T(8,128)(2,1)}, bf16[64,1024]{1,0:T(8,128)(2,1)S(1)}, u32[]{:S(2)}, u32[]{:S(2)}) collective-permute-start(bf16[64,1024]{1,0:T(8,128)(2,1)} %param.11), channel_id=1, source_target_pairs={{0,3},{1,0},{2,1},{3,2},{4,7},{5,4},{6,5},{7,6},{8,11},{9,8},{10,9... | collective-permute-start | bytes 393224 | tf_op jit(solution)/shard_map/ppermute | solution.py:15
  11.6 1.0 copy-start.4
  26.2 1.0 copy-start
  26.3 0.7 copy-start.6
  27.2 1.8 %copy-start.1 = (bf16[1024,256]{1,0:T(8,128)(2,1)S(1)}, bf16[1024,256]{1,0:T(8,128)(2,1)}, u32[]{:S(2)}) copy-start(bf16[1024,256]{1,0:T(8,128)(2,1)} %param.14) | copy-start | bytes 1572868
  27.2 10.2 %collective-permute-start.1 = (bf16[128,1024]{1,0:T(8,128)(2,1)S(1)}, bf16[128,1024]{1,0:T(8,128)(2,1)S(1)}, u32[]{:S(2)}, u32[]{:S(2)}) collective-permute-start(bf16[128,1024]{1,0:T(8,128)(2,1)S(1)} %pad_maximum_fusion), channel_id=1, source_target_pairs={{0,2},{1,3},{2,0},{3,1},{4,6},{5,7},{6,4},{7,5},{8,10},{9,11},{10,... | collective-permute-start | bytes 786440 | tf_op jit(solution)/shard_map/ppermute | solution.py:15
  29.2 1.0 copy-start.2
  68.6 46.8 %reduce-scatter.5.cloned.1.call-start = ((), (), s32[]{:S(2)}) async-start(), calls=%async_computation.2 | async-start | bytes 1310720 | tf_op jit(solution)/shard_map/reduce_scatter | solution.py:135
  74.8 0.8 copy-start.5
  115.3 0.9 copy-start.3
Sparse Core Ops, SparseCore 0:
  68.7 18.7 reduce-scatter.6
  89.9 25.3 reduce-scatter.4
